TPU v7x, 32 devices: a whole 2x2x4 slice. The times are simulated.
32 devices in a mesh: vol: 8 (over z, y), ptcl: 4 (over x, core).
Axes of the slice: x: 2, y: 2, z: 4, core: 2. Of those that a mesh axis runs over, the one named last changes fastest.
Arguments:
- images: bfloat16 [32, 256, 256], P(('vol', 'ptcl')), may hold values from -6 to 6
- defocus: bfloat16 [32], P(('vol', 'ptcl')), may hold values from 20 to 200
- volume: float32 [4096, 256], P('vol'), may hold values from -6 to 6
- counts: int32 [8, 4, 8], P('vol', 'ptcl'), may hold values from 1 to 96, as said below
- slot_pixel: int32 [8, 4, 8, 96], P('vol', 'ptcl'), may hold values from 0 to 511, as said below
- slot_taps: int32 [8, 4, 8, 8, 96], P('vol', 'ptcl'), may hold values from 0 to 511, as said below
- slot_weights: bfloat16 [8, 4, 8, 8, 96], P('vol', 'ptcl'), may hold values from 0.019897461 to 0.25
Outputs:
- volume_next: float32 [4096, 256], P('vol')
Inputs may be any that keep to these rules, and one draw needn't show every extreme that they name: The 8 counts of each holder sum to 512; in each particle shard one owner receives exactly 96 live slots from every holder of that shard. `slot_pixel`: the live slots of a holder (slot index below its count) name each of its 512 pixel blocks exactly once; the other slots hold valid ids. `slot_taps`: the 8 taps of one slot name 8 different blocks.
All inputs are finite; a program needn't handle non-finite values.
Results may differ from a plain program's by a relative error of at most 0.0034.
Values may be sent and summed in bfloat16 or wider, within the bound.
No kernel may reach another device: no remote copies, remote signals or barrier semaphores. Data moves between devices by JAX's collectives and lax.ppermute only.
A program may use at most 64 MiB of HBM per device.

v0:
```python
import math
import jax
import jax.numpy as jnp
from jax import lax
from jax.sharding import PartitionSpec as P

L = 256
BLK = 128
PB = 512
learn_rate = 1.0
phase_shift = 0.1


def dft_tables():
    freq_ids = jnp.arange(L, dtype=jnp.int32)
    product = (freq_ids[:, None] - L // 2) * freq_ids[None, :] % L
    angle = 2.0 * math.pi / L * product.astype(jnp.float32)
    return (jnp.cos(angle).astype(jnp.bfloat16), jnp.sin(angle).astype(jnp.bfloat16))


def transform(pictures, cos_table, sin_table):
    row_cos = jnp.einsum(
        "iyx,kx->iyk", pictures, cos_table, preferred_element_type=jnp.float32
    ).astype(jnp.bfloat16)
    row_sin = jnp.einsum(
        "iyx,kx->iyk", pictures, sin_table, preferred_element_type=jnp.float32
    ).astype(jnp.bfloat16)
    real_part = (
        jnp.einsum("ay,iyb->iab", cos_table, row_cos, preferred_element_type=jnp.float32)
        - jnp.einsum("ay,iyb->iab", sin_table, row_sin, preferred_element_type=jnp.float32)
    ) / L
    imag_part = (
        -(
            jnp.einsum("ay,iyb->iab", sin_table, row_cos, preferred_element_type=jnp.float32)
            + jnp.einsum("ay,iyb->iab", cos_table, row_sin, preferred_element_type=jnp.float32)
        )
        / L
    )
    count_img = pictures.shape[0]
    blocks = jnp.concatenate(
        [real_part.reshape(count_img, PB, BLK), imag_part.reshape(count_img, PB, BLK)], axis=2
    )
    return blocks.reshape(count_img * PB, 2 * BLK).astype(jnp.bfloat16)


def ctf_rows(pixel_ids, focus):
    block_id = pixel_ids % PB
    row_id = block_id // (L // BLK)
    col_id = block_id % (L // BLK) * BLK
    lane_ids = jnp.arange(BLK, dtype=jnp.int32)
    freq_y = (row_id - L // 2).astype(jnp.float32) / L
    freq_x = (col_id[..., None] + lane_ids - L // 2).astype(jnp.float32) / L
    radius = freq_x * freq_x + (freq_y * freq_y)[..., None]
    return -jnp.sin(math.pi * focus.astype(jnp.float32)[..., None] * radius + phase_shift)


def residual_terms(prediction, observed, ctf_values, live_slots):
    shape = prediction.shape
    pred_wide = prediction.astype(jnp.float32).reshape(shape[:-1] + (2, BLK))
    obs_wide = observed.astype(jnp.float32).reshape(shape[:-1] + (2, BLK))
    factor = ctf_values[..., None, :]
    misfit = factor * (factor * pred_wide - obs_wide)
    misfit = jnp.where(live_slots[..., None, None], misfit, 0.0)
    return misfit.reshape(shape).astype(jnp.bfloat16)


def tap_matrix(tap_ids, weights, block_count):
    owners, taps, slots = tap_ids.shape
    flat_taps = jnp.transpose(tap_ids, (0, 2, 1)).reshape(owners * slots, taps)
    flat_weights = jnp.transpose(weights, (0, 2, 1)).reshape(owners * slots, taps)
    block_ids = jnp.arange(block_count, dtype=jnp.int32)
    picked = jnp.where(
        flat_taps[:, :, None] == block_ids[None, None, :],
        flat_weights[:, :, None],
        jnp.zeros((), jnp.bfloat16),
    )
    return jnp.sum(picked, axis=1, dtype=jnp.bfloat16)


def predict_rows(matrix, extract, owners):
    summed = jnp.dot(matrix, extract, preferred_element_type=jnp.float32)
    return summed.reshape(owners, -1, extract.shape[1])


def local(images, defocus, volume, counts, slot_pixel, slot_taps, slot_weights):
    cos_table, sin_table = dft_tables()
    extract = volume.astype(jnp.bfloat16)
    slot_count = counts[0, 0]
    pixel_ids = slot_pixel[0, 0]
    tap_ids = slot_taps[0, 0]
    weights = slot_weights[0, 0]
    owners = pixel_ids.shape[0]
    capacity = pixel_ids.shape[1]
    live_slots = jnp.arange(capacity, dtype=jnp.int32)[None, :] < slot_count[:, None]
    got_taps, got_weights = (
        lax.all_to_all(tap_ids, "vol", split_axis=0, concat_axis=0, tiled=True),
        lax.all_to_all(weights, "vol", split_axis=0, concat_axis=0, tiled=True),
    )
    matrix = tap_matrix(got_taps, got_weights, volume.shape[0])
    prediction = predict_rows(matrix, extract, owners).astype(jnp.bfloat16)
    returned = lax.all_to_all(prediction, "vol", split_axis=0, concat_axis=0, tiled=True)
    observed = transform(images, cos_table, sin_table)
    ctf_values = ctf_rows(pixel_ids, defocus[pixel_ids // PB])
    weighted = residual_terms(returned, observed[pixel_ids], ctf_values, live_slots)
    got_residual = lax.all_to_all(weighted, "vol", split_axis=0, concat_axis=0, tiled=True)
    flat_residual = got_residual.reshape(-1, volume.shape[1])
    gradient = lax.dot_general(
        matrix, flat_residual, (((0,), (0,)), ((), ())), preferred_element_type=jnp.float32
    )
    gradient = lax.psum(gradient, "ptcl")
    return volume - learn_rate * gradient


def solution(mesh):
    placed = (
        P(("vol", "ptcl"), None, None),
        P(("vol", "ptcl")),
        P("vol", None),
        P("vol", "ptcl", None),
        P("vol", "ptcl", None, None),
        P("vol", "ptcl", None, None, None),
        P("vol", "ptcl", None, None, None),
    )
    return jax.shard_map(
        local, mesh=mesh, in_specs=placed, out_specs=P("vol", None), check_vma=False
    )
```

profile of v0, /device:TPU:0, one launch (start us, length us, event | category | flops | bytes accessed | tf_op | source)
XLA Modules:
  0.0 113.2 jit_solution(16446139586523251480)
XLA Ops:
  6.5 7.4 %all-to-all-start.1 = ((bf16[8,8,96]{2,1,0:T(8,128)(2,1)}), bf16[8,8,96]{2,1,0:T(8,128)(2,1)S(1)}, u32[]{:S(2)}, u32[]{:S(2)}) async-start(bf16[8,8,96]{2,1,0:T(8,128)(2,1)} %bitcast.56), calls=%async_computation.1 | async-start | bytes 32768 | tf_op jit(solution)/shard_map/all_to_all | solution.py:97
  14.0 0.7 fusion.29
  14.7 0.7 fusion.25
  15.4 1.1 %convolution_convert_fusion.2 = bf16[256,256]{1,0:T(8,128)(2,1)S(1)} fusion(bf16[1,256,256]{2,1,0:T(8,128)(2,1)S(1)} %copy-done, s32[256]{0:T(256)S(1)} %iota_add_fusion), kind=kOutput, calls=%fused_computation.13 | convolution fusion | flops 34603008 | bytes 263168 | tf_op jit(solution)/shard_map/iyx,kx->iyk/dot_general | solution.py:22
  16.5 1.2 %fusion.23 = f32[256,256]{1,0:T(8,128)S(1)} fusion(bf16[256,256]{1,0:T(8,128)(2,1)S(1)} %convolution_convert_fusion.2, s32[256]{0:T(256)S(1)} %iota_add_fusion), kind=kOutput, calls=%fused_computation.38 | convolution fusion | flops 34537472 | bytes 394240 | tf_op jit(solution)/shard_map/ay,iyb->iab/dot_general | solution.py:34
  17.7 1.2 %fusion.22 = f32[256,256]{1,0:T(8,128)S(1)} fusion(bf16[256,256]{1,0:T(8,128)(2,1)S(1)} %convolution_convert_fusion.2, s32[256]{0:T(256)S(1)} %iota_add_fusion), kind=kOutput, calls=%fused_computation.37 | convolution fusion | flops 34537472 | bytes 394240 | tf_op jit(solution)/shard_map/ay,iyb->iab/dot_general | solution.py:29
  19.6 1.5 %sine_negate_fusion = f32[8,96,128]{2,1,0:T(8,128)S(1)} fusion(f32[8,96]{1,0:T(8,128)S(1)} %fusion.29, s32[8,96]{1,0:T(8,128)S(1)} %fusion.25, f32[]{:T(128)} %bitcast.7), kind=kLoop, calls=%fused_computation.23 | loop fusion | flops 884736 | bytes 399364 | tf_op jit(solution)/shard_map/neg | solution.py:54
  21.1 1.2 %convolution_convert_fusion.1 = bf16[256,256]{1,0:T(8,128)(2,1)S(1)} fusion(bf16[1,256,256]{2,1,0:T(8,128)(2,1)S(1)} %copy-done, s32[256]{0:T(256)S(1)} %iota_add_fusion), kind=kOutput, calls=%fused_computation.12 | convolution fusion | flops 34603008 | bytes 263168 | tf_op jit(solution)/shard_map/iyx,kx->iyk/dot_general | solution.py:25
  22.2 6.0 %all-to-all-start = ((s32[8,8,96]{2,1,0:T(8,128)}), s32[8,8,96]{2,1,0:T(8,128)S(1)}, u32[]{:S(2)}, u32[]{:S(2)}) async-start(s32[8,8,96]{2,1,0:T(8,128)} %bitcast), calls=%async_computation | async-start | bytes 65536 | tf_op jit(solution)/shard_map/all_to_all | solution.py:96
  28.2 1.2 %fusion.7 = bf16[1,256,256]{1,2,0:T(8,128)(2,1)S(1)} fusion(f32[256,256]{1,0:T(8,128)S(1)} %fusion.23, bf16[256,256]{1,0:T(8,128)(2,1)S(1)} %convolution_convert_fusion.1, s32[256]{0:T(256)S(1)} %iota_add_fusion), kind=kOutput, calls=%fused_computation.14 | convolution fusion | flops 34799616 | bytes 525312 | tf_op jit(solution)/shard_map/ay,iyb->iab/dot_general | solution.py:35
  29.6 5.3 %all-to-all-done = s32[8,8,96]{2,1,0:T(8,128)S(1)} async-done(((s32[8,8,96]{2,1,0:T(8,128)}), s32[8,8,96]{2,1,0:T(8,128)S(1)}, u32[]{:S(2)}, u32[]{:S(2)}) %all-to-all-start) | async-done | bytes 24608 | tf_op jit(solution)/shard_map/all_to_all | solution.py:96
  35.1 5.1 %fusion.1 = bf16[768,512]{1,0:T(8,128)(2,1)S(1)} fusion(s32[768,8]{1,0:T(8,128)S(1)} %bitcast.51, bf16[768,8]{1,0:T(8,128)(2,1)S(1)} %bitcast.52), kind=kLoop, calls=%fused_computation.3 | loop fusion | flops 9043968 | bytes 823296 | tf_op jit(solution)/shard_map/reduce_sum | solution.py:77
  40.2 1.1 convolution_convert_fusion
  41.3 4.1 %all-to-all-start.2 = ((bf16[8,96,256]{2,1,0:T(8,128)(2,1)}), bf16[8,96,256]{2,1,0:T(8,128)(2,1)}, u32[]{:S(2)}, u32[]{:S(2)}) async-start(bf16[8,96,256]{2,1,0:T(8,128)(2,1)} %convolution_convert_fusion), calls=%async_computation.2 | async-start | bytes 786432 | tf_op jit(solution)/shard_map/all_to_all | solution.py:101
  45.6 1.2 %fusion.8 = bf16[1,256,256]{1,2,0:T(8,128)(2,1)S(1)} fusion(f32[256,256]{1,0:T(8,128)S(1)} %fusion.22, bf16[256,256]{1,0:T(8,128)(2,1)S(1)} %convolution_convert_fusion.1, s32[256]{0:T(256)S(1)} %iota_add_fusion), kind=kOutput, calls=%fused_computation.15 | convolution fusion | flops 34734080 | bytes 525312 | tf_op jit(solution)/shard_map/ay,iyb->iab/dot_general | solution.py:30
  47.1 0.6 mul.128
  48.1 0.4 copy-done.2
  48.6 2.7 %gather_fusion = bf16[768,256]{1,0:T(8,128)(2,1)S(1)} fusion(bf16[512,256]{1,0:T(8,128)(2,1)S(1)} %maximum_bitcast_fusion, s32[1024]{0:T(1024)S(1)} %pad_clamp_fusion), kind=kCustom, calls=%fused_computation | custom fusion | bytes 789504 | tf_op jit(solution)/shard_map/gather | solution.py:104
  51.3 4.0 %all-to-all-done.2 = bf16[8,96,256]{2,1,0:T(8,128)(2,1)} async-done(((bf16[8,96,256]{2,1,0:T(8,128)(2,1)}), bf16[8,96,256]{2,1,0:T(8,128)(2,1)}, u32[]{:S(2)}, u32[]{:S(2)}) %all-to-all-start.2) | async-done | bytes 393248 | tf_op jit(solution)/shard_map/all_to_all | solution.py:101
  55.4 1.2 %fusion.11 = bf16[8,96,256]{2,1,0:T(8,128)(2,1)S(1)} fusion(f32[8,96,256]{2,1,0:T(8,128)S(1)} %mul.128, bf16[8,96,256]{2,1,0:T(8,128)(2,1)S(1)} %bitcast.50, bf16[8,96,256]{2,1,0:T(8,128)(2,1)} %all-to-all-done.2, pred[8,96]{1,0:T(8,128)(4,1)S(1)} %iota_compare_fusion.1), kind=kLoop, calls=%fused_computation.19 | loop fusion | flops 1376256 | bytes 1966848 | tf_op jit(solution)/shard_map/convert_element_type | solution.py:64
  56.6 14.6 %all_to_all.20 = bf16[8,96,256]{2,1,0:T(8,128)(2,1)S(1)} all-to-all(bf16[8,96,256]{2,1,0:T(8,128)(2,1)S(1)} %fusion.11), channel_id=1, replica_groups=mesh['vol'=8,'ptcl'=4] {'vol'}, dimensions={0} | all-to-all | bytes 786432 | tf_op jit(solution)/shard_map/all_to_all | solution.py:105
  71.2 1.2 %fusion.56 = f32[512,256]{1,0:T(8,128)} fusion(bf16[768,512]{1,0:T(8,128)(2,1)S(1)} %fusion.1, bf16[768,256]{1,0:T(8,128)(2,1)S(1)} %bitcast.53), kind=kOutput, calls=%fused_computation.84 | convolution fusion | flops 201326592 | bytes 1703936 | tf_op jit(solution)/shard_map/dot_general | solution.py:107
  72.4 32.0 %all-reduce.2.cloned.1.call-done = f32[512,256]{1,0:T(8,128)} async-done(((f32[512,256]{1,0:T(8,128)}), f32[512,256]{1,0:T(8,128)}) %all-reduce.2.cloned.1.call-update) | async-done | bytes 524304 | tf_op jit(solution)/shard_map/psum | solution.py:110
  104.4 1.9 %sub.47 = f32[512,256]{1,0:T(8,128)} subtract(f32[512,256]{1,0:T(8,128)S(1)} %copy-done.1, f32[512,256]{1,0:T(8,128)} %all-reduce.2.cloned.1.call-done) | non-fusion elementwise | flops 131072 | bytes 1572864 | tf_op jit(solution)/shard_map/sub | solution.py:111
  (23 shorter events, 1.3 us)
Async XLA Ops:
  6.5 8.8 %copy-start = (bf16[1,256,256]{2,1,0:T(8,128)(2,1)S(1)}, bf16[1,256,256]{2,1,0:T(8,128)(2,1)}, u32[]{:S(2)}) copy-start(bf16[1,256,256]{2,1,0:T(8,128)(2,1)} %param.7) | copy-start | bytes 393220
  6.5 15.7 %all-to-all-start.1 = ((bf16[8,8,96]{2,1,0:T(8,128)(2,1)}), bf16[8,8,96]{2,1,0:T(8,128)(2,1)S(1)}, u32[]{:S(2)}, u32[]{:S(2)}) async-start(bf16[8,8,96]{2,1,0:T(8,128)(2,1)} %bitcast.56), calls=%async_computation.1 | async-start | bytes 32768 | tf_op jit(solution)/shard_map/all_to_all | solution.py:97
  22.2 12.7 %all-to-all-start = ((s32[8,8,96]{2,1,0:T(8,128)}), s32[8,8,96]{2,1,0:T(8,128)S(1)}, u32[]{:S(2)}, u32[]{:S(2)}) async-start(s32[8,8,96]{2,1,0:T(8,128)} %bitcast), calls=%async_computation | async-start | bytes 65536 | tf_op jit(solution)/shard_map/all_to_all | solution.py:96
  35.1 5.1 %copy-start.1 = (f32[512,256]{1,0:T(8,128)S(1)}, f32[512,256]{1,0:T(8,128)}, u32[]{:S(2)}) copy-start(f32[512,256]{1,0:T(8,128)} %param.9) | copy-start | bytes 1572868
  41.3 14.1 %all-to-all-start.2 = ((bf16[8,96,256]{2,1,0:T(8,128)(2,1)}), bf16[8,96,256]{2,1,0:T(8,128)(2,1)}, u32[]{:S(2)}, u32[]{:S(2)}) async-start(bf16[8,96,256]{2,1,0:T(8,128)(2,1)} %convolution_convert_fusion), calls=%async_computation.2 | async-start | bytes 786432 | tf_op jit(solution)/shard_map/all_to_all | solution.py:101
  45.4 59.0 %all-reduce.2.cloned.1.call-start = ((), (), s32[]{:S(2)}) async-start(), calls=%async_computation.4 | async-start | bytes 1048576 | tf_op jit(solution)/shard_map/psum | solution.py:110
  47.8 0.7 copy-start.2
  48.6 2.7 %copy-start.3 = (s32[1,1,8]{2,1,0:T(1,128)S(1)}, s32[1,1,8]{2,1,0:T(1,128)}, u32[]{:S(2)}) copy-start(s32[1,1,8]{2,1,0:T(1,128)} %param.10) | copy-start | bytes 100
Sparse Core Ops, SparseCore 0:
  72.5 31.8 all-reduce.1
where the time goes:
time: 114 us; the launch traced here: 113 us
  waiting for transfers between devices  41.4 us (36%)
  starting transfers between devices  17.7 us (16%)
  blocking collectives  14.6 us (13%)
  between operations  14.2 us (12%)
  other arithmetic  11.1 us (10%)
  matrix products  9.4 us (8%)
  local copies, waits for them, and re-layouts  4.61 us (4%)
    psum x1, waiting for transfers between devices, local(): gradient = lax.psum(gradient, 'ptcl')  32 us
    all_to_all x1, blocking collectives, local(): lax.all_to_all(weighted, 'vol', split_axis=0, concat_axis=0, tiled=True)  14.6 us
    all_to_all x1, starting transfers between devices, local(): lax.all_to_all(weights, 'vol', split_axis=0, concat_axis=0, tiled=True)  7.41 us
    all_to_all x1, starting transfers between devices, local(): lax.all_to_all(tap_ids, 'vol', split_axis=0, concat_axis=0, tiled=True)  6.01 us
    all_to_all x1, waiting for transfers between devices, local(): lax.all_to_all(tap_ids, 'vol', split_axis=0, concat_axis=0, tiled=True)  5.34 us
    reduce_sum x1, other arithmetic, tap_matrix(): return jnp.sum(picked, axis=1, dtype=jnp.bfloat16)  5.06 us
    all_to_all x1, starting transfers between devices, local(): lax.all_to_all(prediction, 'vol', split_axis=0, concat_axis=0, tiled=True)  4.09 us
    all_to_all x1, waiting for transfers between devices, local(): lax.all_to_all(prediction, 'vol', split_axis=0, concat_axis=0, tiled=True)  4.04 us
  transfers between devices with their start and end apart: 4, of which 3 were waited for; matrix products, arithmetic and copies ran while one was open for 13% of the time, Pallas kernels for 0%

commit v1 on v0

--- a/solution.py
+++ b/solution.py
@@ -107,7 +107,8 @@
     gradient = lax.dot_general(
         matrix, flat_residual, (((0,), (0,)), ((), ())), preferred_element_type=jnp.float32
     )
-    gradient = lax.psum(gradient, "ptcl")
+    mixed_arr = jax.lax.all_gather(gradient, "ptcl")
+    gradient = jnp.sum(mixed_arr, 0)
     return volume - learn_rate * gradient
 
 

time: 114 us -> 104 us (0.912)
  waiting for transfers between devices: 41.4 us -> 31.1 us
    psum x1 -> x0, waiting for transfers between devices: 32 us -> none  [local(): gradient = lax.psum(gradient, 'ptcl')]
    all_gather x0 -> x1, waiting for transfers between devices: none -> 21.4 us  [local(): mixed_arr = jax.lax.all_gather(gradient, 'ptcl')]
    reduce_sum x0 -> x1, other arithmetic: none -> 1.79 us  [local(): gradient = jnp.sum(mixed_arr, 0)]
  transfers between devices with their start and end apart: 4 -> 4, of which waited for: 3 -> 3; matrix products, arithmetic and copies ran while one was open for 13% -> 14% of each run, Pallas kernels for 0% -> 0%
where the time goes in v1:
time: 104 us; the launch traced here: 103 us
  waiting for transfers between devices  31.1 us (30%)
  starting transfers between devices  17.7 us (17%)
  blocking collectives  14.6 us (14%)
  between operations  14.3 us (14%)
  other arithmetic  11.9 us (11%)
  matrix products  9.4 us (9%)
  local copies, waits for them, and re-layouts  4.25 us (4%)
    all_gather x1, waiting for transfers between devices, local(): mixed_arr = jax.lax.all_gather(gradient, 'ptcl')  21.4 us
    all_to_all x1, blocking collectives, local(): lax.all_to_all(weighted, 'vol', split_axis=0, concat_axis=0, tiled=True)  14.6 us
    all_to_all x1, starting transfers between devices, local(): lax.all_to_all(weights, 'vol', split_axis=0, concat_axis=0, tiled=True)  7.41 us
    all_to_all x1, starting transfers between devices, local(): lax.all_to_all(tap_ids, 'vol', split_axis=0, concat_axis=0, tiled=True)  6.01 us
    all_to_all x1, waiting for transfers between devices, local(): lax.all_to_all(tap_ids, 'vol', split_axis=0, concat_axis=0, tiled=True)  5.34 us
    reduce_sum x1, other arithmetic, tap_matrix(): return jnp.sum(picked, axis=1, dtype=jnp.bfloat16)  5.06 us
    all_to_all x1, waiting for transfers between devices, local(): lax.all_to_all(prediction, 'vol', split_axis=0, concat_axis=0, tiled=True)  4.38 us
    all_to_all x1, starting transfers between devices, local(): lax.all_to_all(prediction, 'vol', split_axis=0, concat_axis=0, tiled=True)  4.09 us
  transfers between devices with their start and end apart: 4, of which 3 were waited for; matrix products, arithmetic and copies ran while one was open for 14% of the time, Pallas kernels for 0%

profile of v1, /device:TPU:0, one launch (start us, length us, event | category | flops | bytes accessed | tf_op | source)
XLA Modules:
  0.0 103.3 jit_solution(8349849920351582564)
XLA Ops:
  6.5 7.4 %all-to-all-start.1 = ((bf16[8,8,96]{2,1,0:T(8,128)(2,1)}), bf16[8,8,96]{2,1,0:T(8,128)(2,1)S(1)}, u32[]{:S(2)}, u32[]{:S(2)}) async-start(bf16[8,8,96]{2,1,0:T(8,128)(2,1)} %bitcast.58), calls=%async_computation.1 | async-start | bytes 32768 | tf_op jit(solution)/shard_map/all_to_all | solution.py:97
  14.0 0.7 fusion.29
  14.7 0.7 fusion.25
  15.4 1.1 %convolution_convert_fusion.2 = bf16[256,256]{1,0:T(8,128)(2,1)S(1)} fusion(bf16[1,256,256]{2,1,0:T(8,128)(2,1)S(1)} %copy-done, s32[256]{0:T(256)S(1)} %iota_add_fusion), kind=kOutput, calls=%fused_computation.13 | convolution fusion | flops 34603008 | bytes 263168 | tf_op jit(solution)/shard_map/iyx,kx->iyk/dot_general | solution.py:22
  16.5 1.2 %fusion.23 = f32[256,256]{1,0:T(8,128)S(1)} fusion(bf16[256,256]{1,0:T(8,128)(2,1)S(1)} %convolution_convert_fusion.2, s32[256]{0:T(256)S(1)} %iota_add_fusion), kind=kOutput, calls=%fused_computation.38 | convolution fusion | flops 34537472 | bytes 394240 | tf_op jit(solution)/shard_map/ay,iyb->iab/dot_general | solution.py:34
  17.7 1.2 %fusion.22 = f32[256,256]{1,0:T(8,128)S(1)} fusion(bf16[256,256]{1,0:T(8,128)(2,1)S(1)} %convolution_convert_fusion.2, s32[256]{0:T(256)S(1)} %iota_add_fusion), kind=kOutput, calls=%fused_computation.37 | convolution fusion | flops 34537472 | bytes 394240 | tf_op jit(solution)/shard_map/ay,iyb->iab/dot_general | solution.py:29
  19.6 1.5 %sine_negate_fusion = f32[8,96,128]{2,1,0:T(8,128)S(1)} fusion(f32[8,96]{1,0:T(8,128)S(1)} %fusion.29, s32[8,96]{1,0:T(8,128)S(1)} %fusion.25, f32[]{:T(128)} %bitcast.7), kind=kLoop, calls=%fused_computation.23 | loop fusion | flops 884736 | bytes 399364 | tf_op jit(solution)/shard_map/neg | solution.py:54
  21.1 1.2 %convolution_convert_fusion.1 = bf16[256,256]{1,0:T(8,128)(2,1)S(1)} fusion(bf16[1,256,256]{2,1,0:T(8,128)(2,1)S(1)} %copy-done, s32[256]{0:T(256)S(1)} %iota_add_fusion), kind=kOutput, calls=%fused_computation.12 | convolution fusion | flops 34603008 | bytes 263168 | tf_op jit(solution)/shard_map/iyx,kx->iyk/dot_general | solution.py:25
  22.2 6.0 %all-to-all-start = ((s32[8,8,96]{2,1,0:T(8,128)}), s32[8,8,96]{2,1,0:T(8,128)S(1)}, u32[]{:S(2)}, u32[]{:S(2)}) async-start(s32[8,8,96]{2,1,0:T(8,128)} %bitcast), calls=%async_computation | async-start | bytes 65536 | tf_op jit(solution)/shard_map/all_to_all | solution.py:96
  28.3 1.2 %fusion.7 = bf16[1,256,256]{1,2,0:T(8,128)(2,1)S(1)} fusion(f32[256,256]{1,0:T(8,128)S(1)} %fusion.23, bf16[256,256]{1,0:T(8,128)(2,1)S(1)} %convolution_convert_fusion.1, s32[256]{0:T(256)S(1)} %iota_add_fusion), kind=kOutput, calls=%fused_computation.14 | convolution fusion | flops 34799616 | bytes 525312 | tf_op jit(solution)/shard_map/ay,iyb->iab/dot_general | solution.py:35
  29.6 5.3 %all-to-all-done = s32[8,8,96]{2,1,0:T(8,128)S(1)} async-done(((s32[8,8,96]{2,1,0:T(8,128)}), s32[8,8,96]{2,1,0:T(8,128)S(1)}, u32[]{:S(2)}, u32[]{:S(2)}) %all-to-all-start) | async-done | bytes 24608 | tf_op jit(solution)/shard_map/all_to_all | solution.py:96
  35.1 5.1 %fusion.1 = bf16[768,512]{1,0:T(8,128)(2,1)S(1)} fusion(s32[768,8]{1,0:T(8,128)S(1)} %bitcast.53, bf16[768,8]{1,0:T(8,128)(2,1)S(1)} %bitcast.54), kind=kLoop, calls=%fused_computation.3 | loop fusion | flops 9043968 | bytes 823296 | tf_op jit(solution)/shard_map/reduce_sum | solution.py:77
  40.2 1.1 %convolution_convert_fusion = bf16[8,96,256]{2,1,0:T(8,128)(2,1)} fusion(bf16[8,96,512]{2,1,0:T(8,128)(2,1)S(1)} %bitcast.50, f32[512,256]{1,0:T(8,128)S(1)} %copy-done.1), kind=kOutput, calls=%fused_computation.4 | convolution fusion | flops 201654272 | bytes 1703936 | tf_op jit(solution)/shard_map/dot_general | solution.py:81
  41.3 4.1 %all-to-all-start.2 = ((bf16[8,96,256]{2,1,0:T(8,128)(2,1)}), bf16[8,96,256]{2,1,0:T(8,128)(2,1)}, u32[]{:S(2)}, u32[]{:S(2)}) async-start(bf16[8,96,256]{2,1,0:T(8,128)(2,1)} %convolution_convert_fusion), calls=%async_computation.2 | async-start | bytes 786432 | tf_op jit(solution)/shard_map/all_to_all | solution.py:101
  45.6 1.2 %fusion.8 = bf16[1,256,256]{1,2,0:T(8,128)(2,1)S(1)} fusion(f32[256,256]{1,0:T(8,128)S(1)} %fusion.22, bf16[256,256]{1,0:T(8,128)(2,1)S(1)} %convolution_convert_fusion.1, s32[256]{0:T(256)S(1)} %iota_add_fusion), kind=kOutput, calls=%fused_computation.15 | convolution fusion | flops 34734080 | bytes 525312 | tf_op jit(solution)/shard_map/ay,iyb->iab/dot_general | solution.py:30
  47.1 0.6 mul.128
  48.2 2.7 %gather_fusion = bf16[768,256]{1,0:T(8,128)(2,1)S(1)} fusion(bf16[512,256]{1,0:T(8,128)(2,1)S(1)} %maximum_bitcast_fusion, s32[1024]{0:T(1024)S(1)} %pad_clamp_fusion), kind=kCustom, calls=%fused_computation | custom fusion | bytes 789504 | tf_op jit(solution)/shard_map/gather | solution.py:104
  51.0 4.4 %all-to-all-done.2 = bf16[8,96,256]{2,1,0:T(8,128)(2,1)} async-done(((bf16[8,96,256]{2,1,0:T(8,128)(2,1)}), bf16[8,96,256]{2,1,0:T(8,128)(2,1)}, u32[]{:S(2)}, u32[]{:S(2)}) %all-to-all-start.2) | async-done | bytes 393248 | tf_op jit(solution)/shard_map/all_to_all | solution.py:101
  55.4 1.2 %fusion.11 = bf16[8,96,256]{2,1,0:T(8,128)(2,1)S(1)} fusion(f32[8,96,256]{2,1,0:T(8,128)S(1)} %mul.128, bf16[8,96,256]{2,1,0:T(8,128)(2,1)S(1)} %bitcast.52, bf16[8,96,256]{2,1,0:T(8,128)(2,1)} %all-to-all-done.2, pred[8,96]{1,0:T(8,128)(4,1)S(1)} %iota_compare_fusion.1), kind=kLoop, calls=%fused_computation.19 | loop fusion | flops 1376256 | bytes 1966848 | tf_op jit(solution)/shard_map/convert_element_type | solution.py:64
  56.6 14.6 %all_to_all.20 = bf16[8,96,256]{2,1,0:T(8,128)(2,1)S(1)} all-to-all(bf16[8,96,256]{2,1,0:T(8,128)(2,1)S(1)} %fusion.11), channel_id=1, replica_groups=mesh['vol'=8,'ptcl'=4] {'vol'}, dimensions={0} | all-to-all | bytes 786432 | tf_op jit(solution)/shard_map/all_to_all | solution.py:105
  71.2 1.2 %fusion.56 = f32[512,256]{1,0:T(8,128)} fusion(bf16[768,512]{1,0:T(8,128)(2,1)S(1)} %fusion.1, bf16[768,256]{1,0:T(8,128)(2,1)S(1)} %bitcast.55), kind=kOutput, calls=%fused_computation.84 | convolution fusion | flops 201326592 | bytes 1703936 | tf_op jit(solution)/shard_map/dot_general | solution.py:107
  72.4 21.4 %all-gather.3.cloned.1.call-done = f32[2048,256]{1,0:T(8,128)} async-done(((f32[512,256]{1,0:T(8,128)}), f32[2048,256]{1,0:T(8,128)}) %all-gather.3.cloned.1.call-update) | async-done | bytes 2097168 | tf_op jit(solution)/shard_map/all_gather | solution.py:110
  93.8 1.8 %reduce_sum.19 = f32[512,256]{1,0:T(8,128)S(1)} reduce(f32[4,512,256]{2,1,0:T(8,128)} %bitcast.51, f32[]{:T(128)} %constant.86.clone.1), dimensions={0}, to_apply=%region_1.2 | reduce | flops 393216 | bytes 2621444 | tf_op jit(solution)/shard_map/reduce_sum | solution.py:111
  95.6 0.9 sub.47
  (24 shorter events, 1.3 us)
Async XLA Ops:
  6.5 8.8 %copy-start = (bf16[1,256,256]{2,1,0:T(8,128)(2,1)S(1)}, bf16[1,256,256]{2,1,0:T(8,128)(2,1)}, u32[]{:S(2)}) copy-start(bf16[1,256,256]{2,1,0:T(8,128)(2,1)} %param.7) | copy-start | bytes 393220
  6.5 15.7 %all-to-all-start.1 = ((bf16[8,8,96]{2,1,0:T(8,128)(2,1)}), bf16[8,8,96]{2,1,0:T(8,128)(2,1)S(1)}, u32[]{:S(2)}, u32[]{:S(2)}) async-start(bf16[8,8,96]{2,1,0:T(8,128)(2,1)} %bitcast.58), calls=%async_computation.1 | async-start | bytes 32768 | tf_op jit(solution)/shard_map/all_to_all | solution.py:97
  21.1 19.1 %copy-start.1 = (f32[512,256]{1,0:T(8,128)S(1)}, f32[512,256]{1,0:T(8,128)}, u32[]{:S(2)}) copy-start(f32[512,256]{1,0:T(8,128)} %param.9) | copy-start | bytes 1572868
  22.2 12.7 %all-to-all-start = ((s32[8,8,96]{2,1,0:T(8,128)}), s32[8,8,96]{2,1,0:T(8,128)S(1)}, u32[]{:S(2)}, u32[]{:S(2)}) async-start(s32[8,8,96]{2,1,0:T(8,128)} %bitcast), calls=%async_computation | async-start | bytes 65536 | tf_op jit(solution)/shard_map/all_to_all | solution.py:96
  41.3 14.1 %all-to-all-start.2 = ((bf16[8,96,256]{2,1,0:T(8,128)(2,1)}), bf16[8,96,256]{2,1,0:T(8,128)(2,1)}, u32[]{:S(2)}, u32[]{:S(2)}) async-start(bf16[8,96,256]{2,1,0:T(8,128)(2,1)} %convolution_convert_fusion), calls=%async_computation.2 | async-start | bytes 786432 | tf_op jit(solution)/shard_map/all_to_all | solution.py:101
  45.4 48.4 %all-gather.3.cloned.1.call-start = ((), (), s32[]{:S(2)}) async-start(), calls=%async_computation.4 | async-start | bytes 2621440 | tf_op jit(solution)/shard_map/all_gather | solution.py:110
  46.8 1.3 %copy-start.2 = (s32[1,1,8,96]{3,2,1,0:T(8,128)S(1)}, s32[1,1,8,96]{3,2,1,0:T(8,128)}, u32[]{:S(2)}) copy-start(s32[1,1,8,96]{3,2,1,0:T(8,128)} %param.11) | copy-start | bytes 9220
  48.1 2.8 %copy-start.3 = (s32[1,1,8]{2,1,0:T(1,128)S(1)}, s32[1,1,8]{2,1,0:T(1,128)}, u32[]{:S(2)}) copy-start(s32[1,1,8]{2,1,0:T(1,128)} %param.10) | copy-start | bytes 100
Sparse Core Ops, SparseCore 0:
  72.5 21.2 all-gather.2
